TPU v7x, 32 devices: a whole 2x2x4 slice. The times are simulated.
32 devices in a mesh: groups: 2 (over x), seq: 4 (over y, core), pair: 4 (over z).
Axes of the slice: x: 2, y: 2, z: 4, core: 2. Of those that a mesh axis runs over, the one named last changes fastest.
Arguments:
- sequence: bfloat16 [4096, 1536], P(('groups', 'seq', 'pair')), parts along dimension 0, may hold values from -12 to 12
- gain_conv: float32 [1536], replicated, may hold values from 0.25 to 1.75
- conv_weight: bfloat16 [5, 1536, 1536], P(None, 'pair'), may hold values from -0.0625 to 0.0625
- gain_attn: float32 [1536], replicated, may hold values from 0.25 to 1.75
- w_qkv: bfloat16 [1536, 3072], P(None, 'pair'), may hold values from -1 to 1
- w_out: bfloat16 [1024, 1536], P('pair'), may hold values from -0.75 to 0.75
- gain_pool: float32 [1536], replicated, may hold values from 0.25 to 1.75
- w_pair: bfloat16 [1536, 256], replicated, may hold values from -0.15625 to 0.15625
- w_up: bfloat16 [128, 256], replicated, may hold values from -0.5 to 0.5
- w_down: bfloat16 [256, 128], replicated, may hold values from -0.375 to 0.375
Outputs:
- seq_out: bfloat16 [4096, 1536], P(('groups', 'seq', 'pair')), parts along dimension 0
- pair_map: bfloat16 [256, 128, 128], P(('groups', 'seq'), 'pair'), parts along dimension 0
There are 2 independent parts, one for each index of `groups`. A program takes and returns all parts, laid end to end along the dimension named above; an argument that names none is the same for every part. Nothing has to cross between parts.
All inputs are finite; a program needn't handle non-finite values.
Results may differ from a plain program's by a relative error of at most 0.024.
Values may be sent and summed in bfloat16 or wider, within the bound.
No kernel may reach another device: no remote copies, remote signals or barrier semaphores. Data moves between devices by JAX's collectives and lax.ppermute only.
A program may use at most 64 MiB of HBM per device.

v0:
```python
import math
import jax
import jax.numpy as jnp
from jax import lax
from jax.sharding import PartitionSpec as P

KEY_SIZE = 128
VALUE_SIZE = 128
DILATION = 4
POOL = 16
PAIR_CH = 128
EPS = 1e-06


def padded_2(value, sides, width):
    for axis, dim in sides:
        peers, length = (lax.axis_size(axis), value.shape[dim])
        up = [(i, (i + 1) % peers) for i in range(peers - 1)]
        down = [(j, i) for i, j in up]
        last = lax.slice_in_dim(value, length - width, length, axis=dim)
        first = lax.slice_in_dim(value, 0, width, axis=dim)
        before = lax.ppermute(last, axis, up)
        after = lax.ppermute(first, axis, down)
        value = jnp.concatenate([before, value, after], axis=dim)
    return value


def norm_rows(values, gain):
    return values * lax.rsqrt(jnp.mean(values * values, axis=-1, keepdims=True) + EPS) * gain


def conv_rows(padded, conv_weight, row_total):
    summed = jnp.zeros((row_total, conv_weight.shape[2]), jnp.float32)
    for offset in range(conv_weight.shape[0]):
        shifted = lax.dynamic_slice_in_dim(padded, offset * DILATION, row_total, 0)
        summed = summed + jnp.dot(shifted, conv_weight[offset], preferred_element_type=jnp.float32)
    return summed


def line_reduce_scatter(partial, axis):
    n = lax.axis_size(axis)
    me = lax.axis_index(axis)
    rows = partial.shape[0] // n
    blocks = partial.reshape(n, rows, partial.shape[1])
    right = [(i, i + 1) for i in range(n - 1)]
    left = [(i + 1, i) for i in range(n - 1)]
    got_r = jnp.zeros((rows, partial.shape[1]), jnp.bfloat16)
    got_l = jnp.zeros((rows, partial.shape[1]), jnp.bfloat16)
    for step in range(1, n):
        idx_r = jnp.clip(me + n - step, 0, n - 1)
        idx_l = jnp.clip(me - (n - step), 0, n - 1)
        send_r = (blocks[idx_r] + got_r.astype(jnp.float32)).astype(jnp.bfloat16)
        send_l = (blocks[idx_l] + got_l.astype(jnp.float32)).astype(jnp.bfloat16)
        got_r = lax.ppermute(send_r, axis, right)
        got_l = lax.ppermute(send_l, axis, left)
    own = blocks[me]
    return own + got_r.astype(jnp.float32) + got_l.astype(jnp.float32)


def line_all_gather(value, axis):
    n = lax.axis_size(axis)
    me = lax.axis_index(axis)
    rows = value.shape[0]
    right = [(i, i + 1) for i in range(n - 1)]
    left = [(i + 1, i) for i in range(n - 1)]
    slots = jnp.zeros((n + 1, rows) + value.shape[1:], value.dtype)
    slots = lax.dynamic_update_index_in_dim(slots, value, me, 0)
    flow_r, flow_l = (value, value)
    for step in range(1, n):
        flow_r = lax.ppermute(flow_r, axis, right)
        flow_l = lax.ppermute(flow_l, axis, left)
        at_r = jnp.where(me - step >= 0, me - step, n)
        at_l = jnp.where(me + step < n, me + step, n)
        slots = lax.dynamic_update_index_in_dim(slots, flow_r, at_r, 0)
        slots = lax.dynamic_update_index_in_dim(slots, flow_l, at_l, 0)
    return slots[:n].reshape((n * rows,) + value.shape[1:])


def doubling_all_gather(value, axis):
    n = lax.axis_size(axis)
    assert n & n - 1 == 0
    me = lax.axis_index(axis)
    out = value
    k = 1
    while k < n:
        other = lax.ppermute(out, axis, [(i, i ^ k) for i in range(n)])
        low = me & k == 0
        out = jnp.where(low, jnp.concatenate([out, other], 0), jnp.concatenate([other, out], 0))
        k *= 2
    return out


def shards(
    sequence, gain_conv, conv_weight, gain_attn, w_qkv, w_out, gain_pool, w_pair, w_up, w_down
):
    pair_count = lax.axis_size("pair")
    seq_count = lax.axis_size("seq")
    row_count = sequence.shape[0]
    channels = sequence.shape[1]
    local_rows = row_count * pair_count
    inputs = sequence.astype(jnp.float32)
    normed = norm_rows(inputs, gain_conv).astype(jnp.bfloat16)
    swapped = lax.all_to_all(normed, "pair", split_axis=1, concat_axis=0, tiled=True)
    padded = padded_2(swapped, (("seq", 0),), DILATION * (conv_weight.shape[0] - 1) // 2)
    with jax.named_scope("conv_reduce"):
        summed = line_reduce_scatter(conv_rows(padded, conv_weight, local_rows), "pair")
    first_out = (inputs + summed).astype(jnp.bfloat16)
    attn_in = norm_rows(first_out.astype(jnp.float32), gain_attn).astype(jnp.bfloat16)
    with jax.named_scope("attn_in_gather"):
        block_in = line_all_gather(attn_in, "pair")
    projected = jnp.dot(block_in, w_qkv, preferred_element_type=jnp.float32).astype(jnp.bfloat16)
    head_count = projected.shape[1] // (2 * KEY_SIZE + VALUE_SIZE)
    grouped = projected.reshape(local_rows, head_count, 2 * KEY_SIZE + VALUE_SIZE).transpose(
        1, 0, 2
    )
    queries = grouped[:, :, :KEY_SIZE]
    kv = grouped[:, :, KEY_SIZE:]
    scale = 1.0 / math.sqrt(KEY_SIZE)
    ring = [(i, (i + 1) % seq_count) for i in range(seq_count)]

    def attend(state, kv_block):
        running_max, running_sum, weighted = state
        key_block = kv_block[:, :, :KEY_SIZE]
        value_block = kv_block[:, :, KEY_SIZE:]
        scores = (
            jnp.einsum("hqd,hkd->hqk", queries, key_block, preferred_element_type=jnp.float32)
            * scale
        )
        new_max = jnp.maximum(running_max, jnp.max(scores, axis=-1))
        shrink = jnp.exp(running_max - new_max)
        weights = jnp.exp(scores - new_max[:, :, None])
        running_sum = running_sum * shrink + jnp.sum(weights, axis=-1)
        update = jnp.einsum(
            "hqk,hkd->hqd",
            weights.astype(jnp.bfloat16),
            value_block,
            preferred_element_type=jnp.float32,
        )
        weighted = weighted * shrink[:, :, None] + update
        return (new_max, running_sum, weighted)

    state = (
        jnp.full((head_count, local_rows), -1e30, jnp.float32),
        jnp.zeros((head_count, local_rows), jnp.float32),
        jnp.zeros((head_count, local_rows, VALUE_SIZE), jnp.float32),
    )
    with jax.named_scope("kv_ring"):
        current = kv
        for step in range(seq_count):
            if step + 1 < seq_count:
                arriving = lax.ppermute(current, "seq", ring)
            state = attend(state, current)
            if step + 1 < seq_count:
                current = arriving
    running_max, running_sum, weighted = state
    attended = (weighted / running_sum[:, :, None]).astype(jnp.bfloat16)
    attended = attended.transpose(1, 0, 2).reshape(local_rows, head_count * VALUE_SIZE)
    with jax.named_scope("out_reduce"):
        mixed = line_reduce_scatter(
            jnp.dot(attended, w_out, preferred_element_type=jnp.float32), "pair"
        )
    seq_out = (first_out.astype(jnp.float32) + mixed).astype(jnp.bfloat16)
    bin_count = row_count // POOL
    pooled = jnp.mean(seq_out.astype(jnp.float32).reshape(bin_count, POOL, channels), axis=1)
    bin_norm = norm_rows(pooled, gain_pool).astype(jnp.bfloat16)
    sides = jnp.dot(bin_norm, w_pair, preferred_element_type=jnp.float32).astype(jnp.bfloat16)
    with jax.named_scope("sides_gather"):
        all_sides = doubling_all_gather(doubling_all_gather(sides, "pair"), "seq")
    tile_rows = bin_count * pair_count
    tile_cols = bin_count * seq_count
    row_side = lax.dynamic_slice_in_dim(all_sides, lax.axis_index("seq") * tile_rows, tile_rows, 0)[
        :, :PAIR_CH
    ]
    column_side = lax.dynamic_slice_in_dim(
        all_sides, lax.axis_index("pair") * tile_cols, tile_cols, 0
    )[:, PAIR_CH:]
    pair_tile = (
        row_side.astype(jnp.float32)[:, None, :] * column_side.astype(jnp.float32)[None, :, :]
    ).astype(jnp.bfloat16)
    flat_rows = pair_tile.reshape(tile_rows * tile_cols, PAIR_CH)
    hidden = jax.nn.relu(jnp.dot(flat_rows, w_up, preferred_element_type=jnp.float32)).astype(
        jnp.bfloat16
    )
    pair_out = flat_rows.astype(jnp.float32) + jnp.dot(
        hidden, w_down, preferred_element_type=jnp.float32
    )
    pair_map = pair_out.astype(jnp.bfloat16).reshape(tile_rows, tile_cols, PAIR_CH)
    return (seq_out, pair_map)


def solution(mesh):
    return jax.shard_map(
        shards,
        mesh=mesh,
        in_specs=(
            P(("groups", "seq", "pair"), None),
            P(),
            P(None, "pair", None),
            P(),
            P(None, "pair"),
            P("pair", None),
            P(),
            P(),
            P(),
            P(),
        ),
        out_specs=(P(("groups", "seq", "pair"), None), P(("groups", "seq"), "pair", None)),
        check_vma=False,
    )
```

profile of v0, /device:TPU:0, one launch (start us, length us, event | category | flops | bytes accessed | tf_op | source)
XLA Modules:
  0.0 228.1 jit_solution(8391843378703551363)
XLA Ops:
  3.9 6.3 %all-to-all-start = ((bf16[128,4,384]{2,0,1:T(8,128)(2,1)}), bf16[128,4,384]{2,0,1:T(8,128)(2,1)S(1)}, u32[]{:S(2)}, u32[]{:S(2)}) async-start(bf16[128,4,384]{2,0,1:T(8,128)(2,1)} %bitcast.205), calls=%async_computation | async-start | bytes 786432 | tf_op jit(solution)/shard_map/all_to_all | solution.py:103
  10.2 11.7 %all-to-all-done = bf16[128,4,384]{2,0,1:T(8,128)(2,1)S(1)} async-done(((bf16[128,4,384]{2,0,1:T(8,128)(2,1)}), bf16[128,4,384]{2,0,1:T(8,128)(2,1)S(1)}, u32[]{:S(2)}, u32[]{:S(2)}) %all-to-all-start) | async-done | bytes 393248 | tf_op jit(solution)/shard_map/all_to_all | solution.py:103
  38.7 5.8 %collective-permute-done.2 = bf16[128,1536]{1,0:T(8,128)(2,1)} collective-permute-done((bf16[128,1536]{1,0:T(8,128)(2,1)S(1)}, bf16[128,1536]{1,0:T(8,128)(2,1)}, u32[]{:S(2)}, u32[]{:S(2)}) %collective-permute-start.2) | collective-permute-done | bytes 393248 | tf_op jit(solution)/shard_map/conv_reduce/ppermute | solution.py:54
  45.8 5.2 %collective-permute-start.3 = (bf16[128,1536]{1,0:T(8,128)(2,1)S(1)}, bf16[128,1536]{1,0:T(8,128)(2,1)}, u32[]{:S(2)}, u32[]{:S(2)}) collective-permute-start(bf16[128,1536]{1,0:T(8,128)(2,1)S(1)} %fusion.65), channel_id=1, source_target_pairs={{0,1},{1,2},{2,3},{4,5},{5,6},{6,7},{8,9},{9,10},{10,11},{12,13},{... | collective-permute-start | bytes 1179656 | tf_op jit(solution)/shard_map/conv_reduce/ppermute | solution.py:54
  51.1 8.0 %collective-permute-done.3 = bf16[128,1536]{1,0:T(8,128)(2,1)} collective-permute-done((bf16[128,1536]{1,0:T(8,128)(2,1)S(1)}, bf16[128,1536]{1,0:T(8,128)(2,1)}, u32[]{:S(2)}, u32[]{:S(2)}) %collective-permute-start.3) | collective-permute-done | bytes 393248 | tf_op jit(solution)/shard_map/conv_reduce/ppermute | solution.py:54
  62.9 5.9 %collective-permute-start.4 = (bf16[128,1536]{1,0:T(8,128)(2,1)}, bf16[128,1536]{1,0:T(8,128)(2,1)}, u32[]{:S(2)}, u32[]{:S(2)}) collective-permute-start(bf16[128,1536]{1,0:T(8,128)(2,1)} %get-tuple-element.18), channel_id=1, source_target_pairs={{0,1},{1,2},{2,3},{4,5},{5,6},{6,7},{8,9},{9,10},{10,11},{12,13},{... | collective-permute-start | bytes 1179656 | tf_op jit(solution)/shard_map/conv_reduce/ppermute | solution.py:54
  68.8 7.1 %collective-permute-done.6 = bf16[128,1536]{1,0:T(8,128)(2,1)S(1)} collective-permute-done((bf16[128,1536]{1,0:T(8,128)(2,1)S(1)}, bf16[128,1536]{1,0:T(8,128)(2,1)S(1)}, u32[]{:S(2)}, u32[]{:S(2)}) %collective-permute-start.6) | collective-permute-done | bytes 393248 | tf_op jit(solution)/shard_map/conv_reduce/ppermute | solution.py:55
  78.4 11.6 %collective-permute-done.7 = bf16[128,1536]{1,0:T(8,128)(2,1)S(1)} collective-permute-done((bf16[128,1536]{1,0:T(8,128)(2,1)S(1)}, bf16[128,1536]{1,0:T(8,128)(2,1)S(1)}, u32[]{:S(2)}, u32[]{:S(2)}) %collective-permute-start.7) | collective-permute-done | bytes 393248 | tf_op jit(solution)/shard_map/conv_reduce/ppermute | solution.py:55
  94.1 3.6 %collective-permute-start.8 = (bf16[128,1536]{1,0:T(8,128)(2,1)}, bf16[128,1536]{1,0:T(8,128)(2,1)S(1)}, u32[]{:S(2)}, u32[]{:S(2)}) collective-permute-start(bf16[128,1536]{1,0:T(8,128)(2,1)} %get-tuple-element.11), channel_id=1, source_target_pairs={{0,1},{1,2},{2,3},{4,5},{5,6},{6,7},{8,9},{9,10},{10,11},{12,13},{... | collective-permute-start | bytes 1179656 | tf_op jit(solution)/shard_map/attn_in_gather/ppermute | solution.py:70
  99.0 6.5 %collective-permute-done.8 = bf16[128,1536]{1,0:T(8,128)(2,1)S(1)} collective-permute-done((bf16[128,1536]{1,0:T(8,128)(2,1)}, bf16[128,1536]{1,0:T(8,128)(2,1)S(1)}, u32[]{:S(2)}, u32[]{:S(2)}) %collective-permute-start.8) | collective-permute-done | bytes 393248 | tf_op jit(solution)/shard_map/attn_in_gather/ppermute | solution.py:70
  105.5 4.3 %collective-permute-start.10 = (bf16[128,1536]{1,0:T(8,128)(2,1)S(1)}, bf16[128,1536]{1,0:T(8,128)(2,1)S(1)}, u32[]{:S(2)}, u32[]{:S(2)}) collective-permute-start(bf16[128,1536]{1,0:T(8,128)(2,1)S(1)} %collective-permute-done.8), channel_id=1, source_target_pairs={{0,1},{1,2},{2,3},{4,5},{5,6},{6,7},{8,9},{9,10},{10,11},{12,13},{... | collective-permute-start | bytes 1179656 | tf_op jit(solution)/shard_map/attn_in_gather/ppermute | solution.py:70
  112.7 3.8 %collective-permute-done.10 = bf16[128,1536]{1,0:T(8,128)(2,1)S(1)} collective-permute-done((bf16[128,1536]{1,0:T(8,128)(2,1)S(1)}, bf16[128,1536]{1,0:T(8,128)(2,1)S(1)}, u32[]{:S(2)}, u32[]{:S(2)}) %collective-permute-start.10) | collective-permute-done | bytes 393248 | tf_op jit(solution)/shard_map/attn_in_gather/ppermute | solution.py:70
  116.5 4.4 %collective-permute-start.12 = (bf16[128,1536]{1,0:T(8,128)(2,1)S(1)}, bf16[128,1536]{1,0:T(8,128)(2,1)S(1)}, u32[]{:S(2)}, u32[]{:S(2)}) collective-permute-start(bf16[128,1536]{1,0:T(8,128)(2,1)S(1)} %collective-permute-done.10), channel_id=1, source_target_pairs={{0,1},{1,2},{2,3},{4,5},{5,6},{6,7},{8,9},{9,10},{10,11},{12,13},{... | collective-permute-start | bytes 1179656 | tf_op jit(solution)/shard_map/attn_in_gather/ppermute | solution.py:70
  127.4 3.4 %collective-permute-done.13 = bf16[128,1536]{1,0:T(8,128)(2,1)S(1)} collective-permute-done((bf16[128,1536]{1,0:T(8,128)(2,1)S(1)}, bf16[128,1536]{1,0:T(8,128)(2,1)S(1)}, u32[]{:S(2)}, u32[]{:S(2)}) %collective-permute-start.13) | collective-permute-done | bytes 393248 | tf_op jit(solution)/shard_map/attn_in_gather/ppermute | solution.py:71
  134.6 8.6 %collective-permute-done.14 = bf16[2,512,256]{2,1,0:T(8,128)(2,1)S(1)} collective-permute-done((bf16[2,512,256]{2,1,0:T(8,128)(2,1)S(1)}, bf16[2,512,256]{2,1,0:T(8,128)(2,1)S(1)}, u32[]{:S(2)}, u32[]{:S(2)}) %collective-permute-start.14) | collective-permute-done | bytes 524320 | tf_op jit(solution)/shard_map/kv_ring/ppermute | solution.py:151
  143.7 8.2 %collective-permute-done.15 = bf16[2,512,256]{2,1,0:T(8,128)(2,1)S(1)} collective-permute-done((bf16[2,512,256]{2,1,0:T(8,128)(2,1)S(1)}, bf16[2,512,256]{2,1,0:T(8,128)(2,1)S(1)}, u32[]{:S(2)}, u32[]{:S(2)}) %collective-permute-start.15) | collective-permute-done | bytes 524320 | tf_op jit(solution)/shard_map/kv_ring/ppermute | solution.py:151
  152.7 7.7 %collective-permute-done.16 = bf16[2,512,256]{2,1,0:T(8,128)(2,1)S(1)} collective-permute-done((bf16[2,512,256]{2,1,0:T(8,128)(2,1)S(1)}, bf16[2,512,256]{2,1,0:T(8,128)(2,1)S(1)}, u32[]{:S(2)}, u32[]{:S(2)}) %collective-permute-start.16) | collective-permute-done | bytes 524320 | tf_op jit(solution)/shard_map/kv_ring/ppermute | solution.py:151
  171.1 7.1 %collective-permute-done.17 = bf16[128,1536]{1,0:T(8,128)(2,1)S(1)} collective-permute-done((bf16[128,1536]{1,0:T(8,128)(2,1)S(1)}, bf16[128,1536]{1,0:T(8,128)(2,1)S(1)}, u32[]{:S(2)}, u32[]{:S(2)}) %collective-permute-start.17) | collective-permute-done | bytes 393248 | tf_op jit(solution)/shard_map/out_reduce/ppermute | solution.py:54
  178.2 4.4 %collective-permute-start.18 = (bf16[128,1536]{1,0:T(8,128)(2,1)S(1)}, bf16[128,1536]{1,0:T(8,128)(2,1)S(1)}, u32[]{:S(2)}, u32[]{:S(2)}) collective-permute-start(bf16[128,1536]{1,0:T(8,128)(2,1)S(1)} %fusion.58), channel_id=1, source_target_pairs={{0,1},{1,2},{2,3},{4,5},{5,6},{6,7},{8,9},{9,10},{10,11},{12,13},{... | collective-permute-start | bytes 1179656 | tf_op jit(solution)/shard_map/out_reduce/ppermute | solution.py:54
  182.7 7.3 %collective-permute-done.18 = bf16[128,1536]{1,0:T(8,128)(2,1)S(1)} collective-permute-done((bf16[128,1536]{1,0:T(8,128)(2,1)S(1)}, bf16[128,1536]{1,0:T(8,128)(2,1)S(1)}, u32[]{:S(2)}, u32[]{:S(2)}) %collective-permute-start.18) | collective-permute-done | bytes 393248 | tf_op jit(solution)/shard_map/out_reduce/ppermute | solution.py:54
  191.6 5.0 %collective-permute-start.19 = (bf16[128,1536]{1,0:T(8,128)(2,1)S(1)}, bf16[128,1536]{1,0:T(8,128)(2,1)S(1)}, u32[]{:S(2)}, u32[]{:S(2)}) collective-permute-start(bf16[128,1536]{1,0:T(8,128)(2,1)S(1)} %get-tuple-element.14), channel_id=1, source_target_pairs={{0,1},{1,2},{2,3},{4,5},{5,6},{6,7},{8,9},{9,10},{10,11},{12,13},{... | collective-permute-start | bytes 1179656 | tf_op jit(solution)/shard_map/out_reduce/ppermute | solution.py:54
  196.6 5.5 %collective-permute-done.21 = bf16[128,1536]{1,0:T(8,128)(2,1)S(1)} collective-permute-done((bf16[128,1536]{1,0:T(8,128)(2,1)S(1)}, bf16[128,1536]{1,0:T(8,128)(2,1)S(1)}, u32[]{:S(2)}, u32[]{:S(2)}) %collective-permute-start.21) | collective-permute-done | bytes 393248 | tf_op jit(solution)/shard_map/out_reduce/ppermute | solution.py:55
  203.7 8.4 %collective-permute-done.22 = bf16[128,1536]{1,0:T(8,128)(2,1)S(1)} collective-permute-done((bf16[128,1536]{1,0:T(8,128)(2,1)S(1)}, bf16[128,1536]{1,0:T(8,128)(2,1)S(1)}, u32[]{:S(2)}, u32[]{:S(2)}) %collective-permute-start.22) | collective-permute-done | bytes 393248 | tf_op jit(solution)/shard_map/out_reduce/ppermute | solution.py:55
  222.9 3.9 %collective-permute-done.26 = bf16[64,256]{1,0:T(8,128)(2,1)S(1)} collective-permute-done((bf16[64,256]{1,0:T(8,128)(2,1)S(1)}, bf16[64,256]{1,0:T(8,128)(2,1)S(1)}, u32[]{:S(2)}, u32[]{:S(2)}) %collective-permute-start.26) | collective-permute-done | bytes 32800 | tf_op jit(solution)/shard_map/sides_gather/ppermute | solution.py:86
  (108 shorter events, 73.4 us)
Async XLA Ops:
  3.9 18.0 %all-to-all-start = ((bf16[128,4,384]{2,0,1:T(8,128)(2,1)}), bf16[128,4,384]{2,0,1:T(8,128)(2,1)S(1)}, u32[]{:S(2)}, u32[]{:S(2)}) async-start(bf16[128,4,384]{2,0,1:T(8,128)(2,1)} %bitcast.205), calls=%async_computation | async-start | bytes 786432 | tf_op jit(solution)/shard_map/all_to_all | solution.py:103
  21.9 5.3 %collective-permute-start = (bf16[8,384]{1,0:T(8,128)(2,1)S(1)}, bf16[8,384]{1,0:T(8,128)(2,1)S(1)}, u32[]{:S(2)}, u32[]{:S(2)}) collective-permute-start(bf16[8,384]{1,0:T(8,128)(2,1)S(1)} %get-tuple-element.22), channel_id=1, source_target_pairs={{0,4},{4,8},{8,12},{1,5},{5,9},{9,13},{2,6},{6,10},{10,14},{3,7},{... | collective-permute-start | bytes 18440 | tf_op jit(solution)/shard_map/ppermute | solution.py:22
  25.9 4.6 %collective-permute-start.1 = (bf16[8,384]{1,0:T(8,128)(2,1)S(1)}, bf16[8,384]{1,0:T(8,128)(2,1)S(1)}, u32[]{:S(2)}, u32[]{:S(2)}) collective-permute-start(bf16[8,384]{1,0:T(8,128)(2,1)S(1)} %get-tuple-element.23), channel_id=1, source_target_pairs={{4,0},{8,4},{12,8},{5,1},{9,5},{13,9},{6,2},{10,6},{14,10},{7,3},{... | collective-permute-start | bytes 18440 | tf_op jit(solution)/shard_map/ppermute | solution.py:23
  35.2 9.3 %collective-permute-start.2 = (bf16[128,1536]{1,0:T(8,128)(2,1)S(1)}, bf16[128,1536]{1,0:T(8,128)(2,1)}, u32[]{:S(2)}, u32[]{:S(2)}) collective-permute-start(bf16[128,1536]{1,0:T(8,128)(2,1)S(1)} %get-tuple-element.20), channel_id=1, source_target_pairs={{0,1},{1,2},{2,3},{4,5},{5,6},{6,7},{8,9},{9,10},{10,11},{12,13},{... | collective-permute-start | bytes 1179656 | tf_op jit(solution)/shard_map/conv_reduce/ppermute | solution.py:54
  37.4 13.7 %collective-permute-start.5 = (bf16[128,1536]{1,0:T(8,128)(2,1)S(1)}, bf16[128,1536]{1,0:T(8,128)(2,1)}, u32[]{:S(2)}, u32[]{:S(2)}) collective-permute-start(bf16[128,1536]{1,0:T(8,128)(2,1)S(1)} %get-tuple-element.21), channel_id=1, source_target_pairs={{1,0},{2,1},{3,2},{5,4},{6,5},{7,6},{9,8},{10,9},{11,10},{13,12},{... | collective-permute-start | bytes 1179656 | tf_op jit(solution)/shard_map/conv_reduce/ppermute | solution.py:55
  45.8 13.2 %collective-permute-start.3 = (bf16[128,1536]{1,0:T(8,128)(2,1)S(1)}, bf16[128,1536]{1,0:T(8,128)(2,1)}, u32[]{:S(2)}, u32[]{:S(2)}) collective-permute-start(bf16[128,1536]{1,0:T(8,128)(2,1)S(1)} %fusion.65), channel_id=1, source_target_pairs={{0,1},{1,2},{2,3},{4,5},{5,6},{6,7},{8,9},{9,10},{10,11},{12,13},{... | collective-permute-start | bytes 1179656 | tf_op jit(solution)/shard_map/conv_reduce/ppermute | solution.py:54
  61.6 14.3 %collective-permute-start.6 = (bf16[128,1536]{1,0:T(8,128)(2,1)S(1)}, bf16[128,1536]{1,0:T(8,128)(2,1)S(1)}, u32[]{:S(2)}, u32[]{:S(2)}) collective-permute-start(bf16[128,1536]{1,0:T(8,128)(2,1)S(1)} %get-tuple-element.19), channel_id=1, source_target_pairs={{1,0},{2,1},{3,2},{5,4},{6,5},{7,6},{9,8},{10,9},{11,10},{13,12},{... | collective-permute-start | bytes 1179656 | tf_op jit(solution)/shard_map/conv_reduce/ppermute | solution.py:55
  62.9 15.6 %collective-permute-start.4 = (bf16[128,1536]{1,0:T(8,128)(2,1)}, bf16[128,1536]{1,0:T(8,128)(2,1)}, u32[]{:S(2)}, u32[]{:S(2)}) collective-permute-start(bf16[128,1536]{1,0:T(8,128)(2,1)} %get-tuple-element.18), channel_id=1, source_target_pairs={{0,1},{1,2},{2,3},{4,5},{5,6},{6,7},{8,9},{9,10},{10,11},{12,13},{... | collective-permute-start | bytes 1179656 | tf_op jit(solution)/shard_map/conv_reduce/ppermute | solution.py:54
  77.1 12.9 %collective-permute-start.7 = (bf16[128,1536]{1,0:T(8,128)(2,1)S(1)}, bf16[128,1536]{1,0:T(8,128)(2,1)S(1)}, u32[]{:S(2)}, u32[]{:S(2)}) collective-permute-start(bf16[128,1536]{1,0:T(8,128)(2,1)S(1)} %fusion.64), channel_id=1, source_target_pairs={{1,0},{2,1},{3,2},{5,4},{6,5},{7,6},{9,8},{10,9},{11,10},{13,12},{... | collective-permute-start | bytes 1179656 | tf_op jit(solution)/shard_map/conv_reduce/ppermute | solution.py:55
  94.1 11.4 %collective-permute-start.8 = (bf16[128,1536]{1,0:T(8,128)(2,1)}, bf16[128,1536]{1,0:T(8,128)(2,1)S(1)}, u32[]{:S(2)}, u32[]{:S(2)}) collective-permute-start(bf16[128,1536]{1,0:T(8,128)(2,1)} %get-tuple-element.11), channel_id=1, source_target_pairs={{0,1},{1,2},{2,3},{4,5},{5,6},{6,7},{8,9},{9,10},{10,11},{12,13},{... | collective-permute-start | bytes 1179656 | tf_op jit(solution)/shard_map/attn_in_gather/ppermute | solution.py:70
  97.7 12.2 %collective-permute-start.9 = (bf16[128,1536]{1,0:T(8,128)(2,1)}, bf16[128,1536]{1,0:T(8,128)(2,1)S(1)}, u32[]{:S(2)}, u32[]{:S(2)}) collective-permute-start(bf16[128,1536]{1,0:T(8,128)(2,1)} %get-tuple-element.11), channel_id=1, source_target_pairs={{1,0},{2,1},{3,2},{5,4},{6,5},{7,6},{9,8},{10,9},{11,10},{13,12},{... | collective-permute-start | bytes 1179656 | tf_op jit(solution)/shard_map/attn_in_gather/ppermute | solution.py:71
  105.5 10.9 %collective-permute-start.10 = (bf16[128,1536]{1,0:T(8,128)(2,1)S(1)}, bf16[128,1536]{1,0:T(8,128)(2,1)S(1)}, u32[]{:S(2)}, u32[]{:S(2)}) collective-permute-start(bf16[128,1536]{1,0:T(8,128)(2,1)S(1)} %collective-permute-done.8), channel_id=1, source_target_pairs={{0,1},{1,2},{2,3},{4,5},{5,6},{6,7},{8,9},{9,10},{10,11},{12,13},{... | collective-permute-start | bytes 1179656 | tf_op jit(solution)/shard_map/attn_in_gather/ppermute | solution.py:70
  109.9 11.0 %collective-permute-start.11 = (bf16[128,1536]{1,0:T(8,128)(2,1)S(1)}, bf16[128,1536]{1,0:T(8,128)(2,1)S(1)}, u32[]{:S(2)}, u32[]{:S(2)}) collective-permute-start(bf16[128,1536]{1,0:T(8,128)(2,1)S(1)} %collective-permute-done.9), channel_id=1, source_target_pairs={{1,0},{2,1},{3,2},{5,4},{6,5},{7,6},{9,8},{10,9},{11,10},{13,12},{... | collective-permute-start | bytes 1179656 | tf_op jit(solution)/shard_map/attn_in_gather/ppermute | solution.py:71
  116.5 10.1 %collective-permute-start.12 = (bf16[128,1536]{1,0:T(8,128)(2,1)S(1)}, bf16[128,1536]{1,0:T(8,128)(2,1)S(1)}, u32[]{:S(2)}, u32[]{:S(2)}) collective-permute-start(bf16[128,1536]{1,0:T(8,128)(2,1)S(1)} %collective-permute-done.10), channel_id=1, source_target_pairs={{0,1},{1,2},{2,3},{4,5},{5,6},{6,7},{8,9},{9,10},{10,11},{12,13},{... | collective-permute-start | bytes 1179656 | tf_op jit(solution)/shard_map/attn_in_gather/ppermute | solution.py:70
  120.9 9.8 %collective-permute-start.13 = (bf16[128,1536]{1,0:T(8,128)(2,1)S(1)}, bf16[128,1536]{1,0:T(8,128)(2,1)S(1)}, u32[]{:S(2)}, u32[]{:S(2)}) collective-permute-start(bf16[128,1536]{1,0:T(8,128)(2,1)S(1)} %collective-permute-done.11), channel_id=1, source_target_pairs={{1,0},{2,1},{3,2},{5,4},{6,5},{7,6},{9,8},{10,9},{11,10},{13,12},{... | collective-permute-start | bytes 1179656 | tf_op jit(solution)/shard_map/attn_in_gather/ppermute | solution.py:71
  134.6 8.7 %collective-permute-start.14 = (bf16[2,512,256]{2,1,0:T(8,128)(2,1)S(1)}, bf16[2,512,256]{2,1,0:T(8,128)(2,1)S(1)}, u32[]{:S(2)}, u32[]{:S(2)}) collective-permute-start(bf16[2,512,256]{2,1,0:T(8,128)(2,1)S(1)} %slice.92), channel_id=1, source_target_pairs={{0,4},{4,8},{8,12},{12,0},{1,5},{5,9},{9,13},{13,1},{2,6},{6,10},{... | collective-permute-start | bytes 1572872 | tf_op jit(solution)/shard_map/kv_ring/ppermute | solution.py:151
  143.2 8.6 %collective-permute-start.15 = (bf16[2,512,256]{2,1,0:T(8,128)(2,1)S(1)}, bf16[2,512,256]{2,1,0:T(8,128)(2,1)S(1)}, u32[]{:S(2)}, u32[]{:S(2)}) collective-permute-start(bf16[2,512,256]{2,1,0:T(8,128)(2,1)S(1)} %collective-permute-done.14), channel_id=1, source_target_pairs={{0,4},{4,8},{8,12},{12,0},{1,5},{5,9},{9,13},{13,1},{2,6},{6,10},{... | collective-permute-start | bytes 1572872 | tf_op jit(solution)/shard_map/kv_ring/ppermute | solution.py:151
  151.8 8.6 %collective-permute-start.16 = (bf16[2,512,256]{2,1,0:T(8,128)(2,1)S(1)}, bf16[2,512,256]{2,1,0:T(8,128)(2,1)S(1)}, u32[]{:S(2)}, u32[]{:S(2)}) collective-permute-start(bf16[2,512,256]{2,1,0:T(8,128)(2,1)S(1)} %collective-permute-done.15), channel_id=1, source_target_pairs={{0,4},{4,8},{8,12},{12,0},{1,5},{5,9},{9,13},{13,1},{2,6},{6,10},{... | collective-permute-start | bytes 1572872 | tf_op jit(solution)/shard_map/kv_ring/ppermute | solution.py:151
  167.5 10.6 %collective-permute-start.17 = (bf16[128,1536]{1,0:T(8,128)(2,1)S(1)}, bf16[128,1536]{1,0:T(8,128)(2,1)S(1)}, u32[]{:S(2)}, u32[]{:S(2)}) collective-permute-start(bf16[128,1536]{1,0:T(8,128)(2,1)S(1)} %get-tuple-element.16), channel_id=1, source_target_pairs={{0,1},{1,2},{2,3},{4,5},{5,6},{6,7},{8,9},{9,10},{10,11},{12,13},{... | collective-permute-start | bytes 1179656 | tf_op jit(solution)/shard_map/out_reduce/ppermute | solution.py:54
  169.8 12.9 %collective-permute-start.20 = (bf16[128,1536]{1,0:T(8,128)(2,1)S(1)}, bf16[128,1536]{1,0:T(8,128)(2,1)S(1)}, u32[]{:S(2)}, u32[]{:S(2)}) collective-permute-start(bf16[128,1536]{1,0:T(8,128)(2,1)S(1)} %get-tuple-element.17), channel_id=1, source_target_pairs={{1,0},{2,1},{3,2},{5,4},{6,5},{7,6},{9,8},{10,9},{11,10},{13,12},{... | collective-permute-start | bytes 1179656 | tf_op jit(solution)/shard_map/out_reduce/ppermute | solution.py:55
  178.2 11.7 %collective-permute-start.18 = (bf16[128,1536]{1,0:T(8,128)(2,1)S(1)}, bf16[128,1536]{1,0:T(8,128)(2,1)S(1)}, u32[]{:S(2)}, u32[]{:S(2)}) collective-permute-start(bf16[128,1536]{1,0:T(8,128)(2,1)S(1)} %fusion.58), channel_id=1, source_target_pairs={{0,1},{1,2},{2,3},{4,5},{5,6},{6,7},{8,9},{9,10},{10,11},{12,13},{... | collective-permute-start | bytes 1179656 | tf_op jit(solution)/shard_map/out_reduce/ppermute | solution.py:54
  190.1 12.0 %collective-permute-start.21 = (bf16[128,1536]{1,0:T(8,128)(2,1)S(1)}, bf16[128,1536]{1,0:T(8,128)(2,1)S(1)}, u32[]{:S(2)}, u32[]{:S(2)}) collective-permute-start(bf16[128,1536]{1,0:T(8,128)(2,1)S(1)} %get-tuple-element.15), channel_id=1, source_target_pairs={{1,0},{2,1},{3,2},{5,4},{6,5},{7,6},{9,8},{10,9},{11,10},{13,12},{... | collective-permute-start | bytes 1179656 | tf_op jit(solution)/shard_map/out_reduce/ppermute | solution.py:55
  191.6 12.1 %collective-permute-start.19 = (bf16[128,1536]{1,0:T(8,128)(2,1)S(1)}, bf16[128,1536]{1,0:T(8,128)(2,1)S(1)}, u32[]{:S(2)}, u32[]{:S(2)}) collective-permute-start(bf16[128,1536]{1,0:T(8,128)(2,1)S(1)} %get-tuple-element.14), channel_id=1, source_target_pairs={{0,1},{1,2},{2,3},{4,5},{5,6},{6,7},{8,9},{9,10},{10,11},{12,13},{... | collective-permute-start | bytes 1179656 | tf_op jit(solution)/shard_map/out_reduce/ppermute | solution.py:54
  202.2 9.8 %collective-permute-start.22 = (bf16[128,1536]{1,0:T(8,128)(2,1)S(1)}, bf16[128,1536]{1,0:T(8,128)(2,1)S(1)}, u32[]{:S(2)}, u32[]{:S(2)}) collective-permute-start(bf16[128,1536]{1,0:T(8,128)(2,1)S(1)} %fusion.57), channel_id=1, source_target_pairs={{1,0},{2,1},{3,2},{5,4},{6,5},{7,6},{9,8},{10,9},{11,10},{13,12},{... | collective-permute-start | bytes 1179656 | tf_op jit(solution)/shard_map/out_reduce/ppermute | solution.py:55
  (13 other events, 301.6 us)
where the time goes:
time: 229 us; the launch traced here: 228 us
  waiting for transfers between devices  125 us (55%)
  starting transfers between devices  62.1 us (27%)
  matrix products  15.6 us (7%)
  other arithmetic  13.1 us (6%)
  local copies, waits for them, and re-layouts  10.8 us (5%)
    ppermute x6, waiting for transfers between devices, line_reduce_scatter(): got_l = lax.ppermute(send_l, axis, left)  32.6 us
    ppermute x6, waiting for transfers between devices, line_reduce_scatter(): got_r = lax.ppermute(send_r, axis, right)  28.1 us
    ppermute x6, starting transfers between devices, line_reduce_scatter(): got_r = lax.ppermute(send_r, axis, right)  25 us
    ppermute x3, waiting for transfers between devices, shards(): arriving = lax.ppermute(current, 'seq', ring)  24.4 us
    ppermute x3, waiting for transfers between devices, line_all_gather(): flow_r = lax.ppermute(flow_r, axis, right)  13.1 us
    ppermute x3, starting transfers between devices, line_all_gather(): flow_r = lax.ppermute(flow_r, axis, right)  12.2 us
    all_to_all x1, waiting for transfers between devices, shards(): lax.all_to_all(normed, 'pair', split_axis=1, concat_axis=0, tiled=True)  11.7 us
    ppermute x4, waiting for transfers between devices, doubling_all_gather(): other = lax.ppermute(out, axis, [(i, i ^ k) for i in range(n)])  9.48 us
  transfers between devices with their start and end apart: 28, of which 21 were waited for; matrix products, arithmetic and copies ran while one was open for 5% of the time, Pallas kernels for 0%

commit v1 on v0

--- a/solution.py
+++ b/solution.py
@@ -100,7 +100,10 @@
     local_rows = row_count * pair_count
     inputs = sequence.astype(jnp.float32)
     normed = norm_rows(inputs, gain_conv).astype(jnp.bfloat16)
-    swapped = lax.all_to_all(normed, "pair", split_axis=1, concat_axis=0, tiled=True)
+    swapped = jnp.concatenate(
+        lax.all_to_all(jnp.stack(jnp.split(normed, lax.axis_size("pair"), axis=1)), "pair", 0, 0),
+        axis=0,
+    )
     padded = padded_2(swapped, (("seq", 0),), DILATION * (conv_weight.shape[0] - 1) // 2)
     with jax.named_scope("conv_reduce"):
         summed = line_reduce_scatter(conv_rows(padded, conv_weight, local_rows), "pair")

time: 229 us -> 229 us (level)
  no operation moved by 1% of the time
where the time goes in v1:
time: 229 us; the launch traced here: 228 us
  waiting for transfers between devices  125 us (55%)
  starting transfers between devices  62.2 us (27%)
  matrix products  15.6 us (7%)
  other arithmetic  14 us (6%)
  local copies, waits for them, and re-layouts  10.2 us (4%)
    ppermute x6, waiting for transfers between devices, line_reduce_scatter(): got_l = lax.ppermute(send_l, axis, left)  32.6 us
    ppermute x6, waiting for transfers between devices, line_reduce_scatter(): got_r = lax.ppermute(send_r, axis, right)  28.1 us
    ppermute x6, starting transfers between devices, line_reduce_scatter(): got_r = lax.ppermute(send_r, axis, right)  25 us
    ppermute x3, waiting for transfers between devices, shards(): arriving = lax.ppermute(current, 'seq', ring)  24.4 us
    ppermute x3, waiting for transfers between devices, line_all_gather(): flow_r = lax.ppermute(flow_r, axis, right)  13.1 us
    ppermute x3, starting transfers between devices, line_all_gather(): flow_r = lax.ppermute(flow_r, axis, right)  12.2 us
    all_to_all x1, waiting for transfers between devices, shards(): lax.all_to_all(jnp.stack(jnp.split(normed, lax.axis_size('pair'), axis=1)...  11.7 us
    ppermute x4, waiting for transfers between devices, doubling_all_gather(): other = lax.ppermute(out, axis, [(i, i ^ k) for i in range(n)])  9.4 us
  transfers between devices with their start and end apart: 28, of which 21 were waited for; matrix products, arithmetic and copies ran while one was open for 5% of the time, Pallas kernels for 0%

profile of v1, /device:TPU:0, one launch (start us, length us, event | category | flops | bytes accessed | tf_op | source)
XLA Modules:
  0.0 228.2 jit_solution(12920656637107736659)
XLA Ops:
  4.0 6.3 %all-to-all-start = ((bf16[4,128,384]{2,1,0:T(8,128)(2,1)}), bf16[4,128,384]{2,1,0:T(8,128)(2,1)S(1)}, u32[]{:S(2)}, u32[]{:S(2)}) async-start(bf16[4,128,384]{2,1,0:T(8,128)(2,1)} %pad_maximum_fusion.4), calls=%async_computation | async-start | bytes 786432 | tf_op jit(solution)/shard_map/all_to_all | solution.py:104
  10.3 11.7 %all-to-all-done = bf16[4,128,384]{2,1,0:T(8,128)(2,1)S(1)} async-done(((bf16[4,128,384]{2,1,0:T(8,128)(2,1)}), bf16[4,128,384]{2,1,0:T(8,128)(2,1)S(1)}, u32[]{:S(2)}, u32[]{:S(2)}) %all-to-all-start) | async-done | bytes 393248 | tf_op jit(solution)/shard_map/all_to_all | solution.py:104
  38.8 5.8 %collective-permute-done.2 = bf16[128,1536]{1,0:T(8,128)(2,1)} collective-permute-done((bf16[128,1536]{1,0:T(8,128)(2,1)S(1)}, bf16[128,1536]{1,0:T(8,128)(2,1)}, u32[]{:S(2)}, u32[]{:S(2)}) %collective-permute-start.2) | collective-permute-done | bytes 393248 | tf_op jit(solution)/shard_map/conv_reduce/ppermute | solution.py:54
  45.9 5.2 %collective-permute-start.3 = (bf16[128,1536]{1,0:T(8,128)(2,1)S(1)}, bf16[128,1536]{1,0:T(8,128)(2,1)}, u32[]{:S(2)}, u32[]{:S(2)}) collective-permute-start(bf16[128,1536]{1,0:T(8,128)(2,1)S(1)} %fusion.65), channel_id=1, source_target_pairs={{0,1},{1,2},{2,3},{4,5},{5,6},{6,7},{8,9},{9,10},{10,11},{12,13},{... | collective-permute-start | bytes 1179656 | tf_op jit(solution)/shard_map/conv_reduce/ppermute | solution.py:54
  51.2 8.0 %collective-permute-done.3 = bf16[128,1536]{1,0:T(8,128)(2,1)} collective-permute-done((bf16[128,1536]{1,0:T(8,128)(2,1)S(1)}, bf16[128,1536]{1,0:T(8,128)(2,1)}, u32[]{:S(2)}, u32[]{:S(2)}) %collective-permute-start.3) | collective-permute-done | bytes 393248 | tf_op jit(solution)/shard_map/conv_reduce/ppermute | solution.py:54
  62.9 5.9 %collective-permute-start.4 = (bf16[128,1536]{1,0:T(8,128)(2,1)}, bf16[128,1536]{1,0:T(8,128)(2,1)}, u32[]{:S(2)}, u32[]{:S(2)}) collective-permute-start(bf16[128,1536]{1,0:T(8,128)(2,1)} %get-tuple-element.18), channel_id=1, source_target_pairs={{0,1},{1,2},{2,3},{4,5},{5,6},{6,7},{8,9},{9,10},{10,11},{12,13},{... | collective-permute-start | bytes 1179656 | tf_op jit(solution)/shard_map/conv_reduce/ppermute | solution.py:54
  68.9 7.1 %collective-permute-done.6 = bf16[128,1536]{1,0:T(8,128)(2,1)S(1)} collective-permute-done((bf16[128,1536]{1,0:T(8,128)(2,1)S(1)}, bf16[128,1536]{1,0:T(8,128)(2,1)S(1)}, u32[]{:S(2)}, u32[]{:S(2)}) %collective-permute-start.6) | collective-permute-done | bytes 393248 | tf_op jit(solution)/shard_map/conv_reduce/ppermute | solution.py:55
  78.5 11.6 %collective-permute-done.7 = bf16[128,1536]{1,0:T(8,128)(2,1)S(1)} collective-permute-done((bf16[128,1536]{1,0:T(8,128)(2,1)S(1)}, bf16[128,1536]{1,0:T(8,128)(2,1)S(1)}, u32[]{:S(2)}, u32[]{:S(2)}) %collective-permute-start.7) | collective-permute-done | bytes 393248 | tf_op jit(solution)/shard_map/conv_reduce/ppermute | solution.py:55
  94.2 3.6 %collective-permute-start.8 = (bf16[128,1536]{1,0:T(8,128)(2,1)}, bf16[128,1536]{1,0:T(8,128)(2,1)S(1)}, u32[]{:S(2)}, u32[]{:S(2)}) collective-permute-start(bf16[128,1536]{1,0:T(8,128)(2,1)} %get-tuple-element.11), channel_id=1, source_target_pairs={{0,1},{1,2},{2,3},{4,5},{5,6},{6,7},{8,9},{9,10},{10,11},{12,13},{... | collective-permute-start | bytes 1179656 | tf_op jit(solution)/shard_map/attn_in_gather/ppermute | solution.py:70
  99.1 6.5 %collective-permute-done.8 = bf16[128,1536]{1,0:T(8,128)(2,1)S(1)} collective-permute-done((bf16[128,1536]{1,0:T(8,128)(2,1)}, bf16[128,1536]{1,0:T(8,128)(2,1)S(1)}, u32[]{:S(2)}, u32[]{:S(2)}) %collective-permute-start.8) | collective-permute-done | bytes 393248 | tf_op jit(solution)/shard_map/attn_in_gather/ppermute | solution.py:70
  105.6 4.3 %collective-permute-start.10 = (bf16[128,1536]{1,0:T(8,128)(2,1)S(1)}, bf16[128,1536]{1,0:T(8,128)(2,1)S(1)}, u32[]{:S(2)}, u32[]{:S(2)}) collective-permute-start(bf16[128,1536]{1,0:T(8,128)(2,1)S(1)} %collective-permute-done.8), channel_id=1, source_target_pairs={{0,1},{1,2},{2,3},{4,5},{5,6},{6,7},{8,9},{9,10},{10,11},{12,13},{... | collective-permute-start | bytes 1179656 | tf_op jit(solution)/shard_map/attn_in_gather/ppermute | solution.py:70
  112.8 3.8 %collective-permute-done.10 = bf16[128,1536]{1,0:T(8,128)(2,1)S(1)} collective-permute-done((bf16[128,1536]{1,0:T(8,128)(2,1)S(1)}, bf16[128,1536]{1,0:T(8,128)(2,1)S(1)}, u32[]{:S(2)}, u32[]{:S(2)}) %collective-permute-start.10) | collective-permute-done | bytes 393248 | tf_op jit(solution)/shard_map/attn_in_gather/ppermute | solution.py:70
  116.6 4.4 %collective-permute-start.12 = (bf16[128,1536]{1,0:T(8,128)(2,1)S(1)}, bf16[128,1536]{1,0:T(8,128)(2,1)S(1)}, u32[]{:S(2)}, u32[]{:S(2)}) collective-permute-start(bf16[128,1536]{1,0:T(8,128)(2,1)S(1)} %collective-permute-done.10), channel_id=1, source_target_pairs={{0,1},{1,2},{2,3},{4,5},{5,6},{6,7},{8,9},{9,10},{10,11},{12,13},{... | collective-permute-start | bytes 1179656 | tf_op jit(solution)/shard_map/attn_in_gather/ppermute | solution.py:70
  127.5 3.4 %collective-permute-done.13 = bf16[128,1536]{1,0:T(8,128)(2,1)S(1)} collective-permute-done((bf16[128,1536]{1,0:T(8,128)(2,1)S(1)}, bf16[128,1536]{1,0:T(8,128)(2,1)S(1)}, u32[]{:S(2)}, u32[]{:S(2)}) %collective-permute-start.13) | collective-permute-done | bytes 393248 | tf_op jit(solution)/shard_map/attn_in_gather/ppermute | solution.py:71
  134.7 8.6 %collective-permute-done.14 = bf16[2,512,256]{2,1,0:T(8,128)(2,1)S(1)} collective-permute-done((bf16[2,512,256]{2,1,0:T(8,128)(2,1)S(1)}, bf16[2,512,256]{2,1,0:T(8,128)(2,1)S(1)}, u32[]{:S(2)}, u32[]{:S(2)}) %collective-permute-start.14) | collective-permute-done | bytes 524320 | tf_op jit(solution)/shard_map/kv_ring/ppermute | solution.py:154
  143.8 8.2 %collective-permute-done.15 = bf16[2,512,256]{2,1,0:T(8,128)(2,1)S(1)} collective-permute-done((bf16[2,512,256]{2,1,0:T(8,128)(2,1)S(1)}, bf16[2,512,256]{2,1,0:T(8,128)(2,1)S(1)}, u32[]{:S(2)}, u32[]{:S(2)}) %collective-permute-start.15) | collective-permute-done | bytes 524320 | tf_op jit(solution)/shard_map/kv_ring/ppermute | solution.py:154
  152.8 7.7 %collective-permute-done.16 = bf16[2,512,256]{2,1,0:T(8,128)(2,1)S(1)} collective-permute-done((bf16[2,512,256]{2,1,0:T(8,128)(2,1)S(1)}, bf16[2,512,256]{2,1,0:T(8,128)(2,1)S(1)}, u32[]{:S(2)}, u32[]{:S(2)}) %collective-permute-start.16) | collective-permute-done | bytes 524320 | tf_op jit(solution)/shard_map/kv_ring/ppermute | solution.py:154
  171.2 7.1 %collective-permute-done.17 = bf16[128,1536]{1,0:T(8,128)(2,1)S(1)} collective-permute-done((bf16[128,1536]{1,0:T(8,128)(2,1)S(1)}, bf16[128,1536]{1,0:T(8,128)(2,1)S(1)}, u32[]{:S(2)}, u32[]{:S(2)}) %collective-permute-start.17) | collective-permute-done | bytes 393248 | tf_op jit(solution)/shard_map/out_reduce/ppermute | solution.py:54
  178.4 4.4 %collective-permute-start.18 = (bf16[128,1536]{1,0:T(8,128)(2,1)S(1)}, bf16[128,1536]{1,0:T(8,128)(2,1)S(1)}, u32[]{:S(2)}, u32[]{:S(2)}) collective-permute-start(bf16[128,1536]{1,0:T(8,128)(2,1)S(1)} %fusion.58), channel_id=1, source_target_pairs={{0,1},{1,2},{2,3},{4,5},{5,6},{6,7},{8,9},{9,10},{10,11},{12,13},{... | collective-permute-start | bytes 1179656 | tf_op jit(solution)/shard_map/out_reduce/ppermute | solution.py:54
  182.8 7.3 %collective-permute-done.18 = bf16[128,1536]{1,0:T(8,128)(2,1)S(1)} collective-permute-done((bf16[128,1536]{1,0:T(8,128)(2,1)S(1)}, bf16[128,1536]{1,0:T(8,128)(2,1)S(1)}, u32[]{:S(2)}, u32[]{:S(2)}) %collective-permute-start.18) | collective-permute-done | bytes 393248 | tf_op jit(solution)/shard_map/out_reduce/ppermute | solution.py:54
  191.7 5.0 %collective-permute-start.19 = (bf16[128,1536]{1,0:T(8,128)(2,1)S(1)}, bf16[128,1536]{1,0:T(8,128)(2,1)S(1)}, u32[]{:S(2)}, u32[]{:S(2)}) collective-permute-start(bf16[128,1536]{1,0:T(8,128)(2,1)S(1)} %get-tuple-element.14), channel_id=1, source_target_pairs={{0,1},{1,2},{2,3},{4,5},{5,6},{6,7},{8,9},{9,10},{10,11},{12,13},{... | collective-permute-start | bytes 1179656 | tf_op jit(solution)/shard_map/out_reduce/ppermute | solution.py:54
  196.7 5.5 %collective-permute-done.21 = bf16[128,1536]{1,0:T(8,128)(2,1)S(1)} collective-permute-done((bf16[128,1536]{1,0:T(8,128)(2,1)S(1)}, bf16[128,1536]{1,0:T(8,128)(2,1)S(1)}, u32[]{:S(2)}, u32[]{:S(2)}) %collective-permute-start.21) | collective-permute-done | bytes 393248 | tf_op jit(solution)/shard_map/out_reduce/ppermute | solution.py:55
  203.8 8.4 %collective-permute-done.22 = bf16[128,1536]{1,0:T(8,128)(2,1)S(1)} collective-permute-done((bf16[128,1536]{1,0:T(8,128)(2,1)S(1)}, bf16[128,1536]{1,0:T(8,128)(2,1)S(1)}, u32[]{:S(2)}, u32[]{:S(2)}) %collective-permute-start.22) | collective-permute-done | bytes 393248 | tf_op jit(solution)/shard_map/out_reduce/ppermute | solution.py:55
  223.1 3.8 %collective-permute-done.26 = bf16[64,256]{1,0:T(8,128)(2,1)S(1)} collective-permute-done((bf16[64,256]{1,0:T(8,128)(2,1)S(1)}, bf16[64,256]{1,0:T(8,128)(2,1)S(1)}, u32[]{:S(2)}, u32[]{:S(2)}) %collective-permute-start.26) | collective-permute-done | bytes 32800 | tf_op jit(solution)/shard_map/sides_gather/ppermute | solution.py:86
  (109 shorter events, 73.6 us)
Async XLA Ops:
  4.0 18.0 %all-to-all-start = ((bf16[4,128,384]{2,1,0:T(8,128)(2,1)}), bf16[4,128,384]{2,1,0:T(8,128)(2,1)S(1)}, u32[]{:S(2)}, u32[]{:S(2)}) async-start(bf16[4,128,384]{2,1,0:T(8,128)(2,1)} %pad_maximum_fusion.4), calls=%async_computation | async-start | bytes 786432 | tf_op jit(solution)/shard_map/all_to_all | solution.py:104
  22.0 5.3 %collective-permute-start = (bf16[8,384]{1,0:T(8,128)(2,1)S(1)}, bf16[8,384]{1,0:T(8,128)(2,1)S(1)}, u32[]{:S(2)}, u32[]{:S(2)}) collective-permute-start(bf16[8,384]{1,0:T(8,128)(2,1)S(1)} %get-tuple-element.22), channel_id=1, source_target_pairs={{0,4},{4,8},{8,12},{1,5},{5,9},{9,13},{2,6},{6,10},{10,14},{3,7},{... | collective-permute-start | bytes 18440 | tf_op jit(solution)/shard_map/ppermute | solution.py:22
  26.0 4.7 %collective-permute-start.1 = (bf16[8,384]{1,0:T(8,128)(2,1)S(1)}, bf16[8,384]{1,0:T(8,128)(2,1)S(1)}, u32[]{:S(2)}, u32[]{:S(2)}) collective-permute-start(bf16[8,384]{1,0:T(8,128)(2,1)S(1)} %get-tuple-element.23), channel_id=1, source_target_pairs={{4,0},{8,4},{12,8},{5,1},{9,5},{13,9},{6,2},{10,6},{14,10},{7,3},{... | collective-permute-start | bytes 18440 | tf_op jit(solution)/shard_map/ppermute | solution.py:23
  35.3 9.3 %collective-permute-start.2 = (bf16[128,1536]{1,0:T(8,128)(2,1)S(1)}, bf16[128,1536]{1,0:T(8,128)(2,1)}, u32[]{:S(2)}, u32[]{:S(2)}) collective-permute-start(bf16[128,1536]{1,0:T(8,128)(2,1)S(1)} %get-tuple-element.20), channel_id=1, source_target_pairs={{0,1},{1,2},{2,3},{4,5},{5,6},{6,7},{8,9},{9,10},{10,11},{12,13},{... | collective-permute-start | bytes 1179656 | tf_op jit(solution)/shard_map/conv_reduce/ppermute | solution.py:54
  37.5 13.7 %collective-permute-start.5 = (bf16[128,1536]{1,0:T(8,128)(2,1)S(1)}, bf16[128,1536]{1,0:T(8,128)(2,1)}, u32[]{:S(2)}, u32[]{:S(2)}) collective-permute-start(bf16[128,1536]{1,0:T(8,128)(2,1)S(1)} %get-tuple-element.21), channel_id=1, source_target_pairs={{1,0},{2,1},{3,2},{5,4},{6,5},{7,6},{9,8},{10,9},{11,10},{13,12},{... | collective-permute-start | bytes 1179656 | tf_op jit(solution)/shard_map/conv_reduce/ppermute | solution.py:55
  45.9 13.2 %collective-permute-start.3 = (bf16[128,1536]{1,0:T(8,128)(2,1)S(1)}, bf16[128,1536]{1,0:T(8,128)(2,1)}, u32[]{:S(2)}, u32[]{:S(2)}) collective-permute-start(bf16[128,1536]{1,0:T(8,128)(2,1)S(1)} %fusion.65), channel_id=1, source_target_pairs={{0,1},{1,2},{2,3},{4,5},{5,6},{6,7},{8,9},{9,10},{10,11},{12,13},{... | collective-permute-start | bytes 1179656 | tf_op jit(solution)/shard_map/conv_reduce/ppermute | solution.py:54
  61.7 14.3 %collective-permute-start.6 = (bf16[128,1536]{1,0:T(8,128)(2,1)S(1)}, bf16[128,1536]{1,0:T(8,128)(2,1)S(1)}, u32[]{:S(2)}, u32[]{:S(2)}) collective-permute-start(bf16[128,1536]{1,0:T(8,128)(2,1)S(1)} %get-tuple-element.19), channel_id=1, source_target_pairs={{1,0},{2,1},{3,2},{5,4},{6,5},{7,6},{9,8},{10,9},{11,10},{13,12},{... | collective-permute-start | bytes 1179656 | tf_op jit(solution)/shard_map/conv_reduce/ppermute | solution.py:55
  62.9 15.6 %collective-permute-start.4 = (bf16[128,1536]{1,0:T(8,128)(2,1)}, bf16[128,1536]{1,0:T(8,128)(2,1)}, u32[]{:S(2)}, u32[]{:S(2)}) collective-permute-start(bf16[128,1536]{1,0:T(8,128)(2,1)} %get-tuple-element.18), channel_id=1, source_target_pairs={{0,1},{1,2},{2,3},{4,5},{5,6},{6,7},{8,9},{9,10},{10,11},{12,13},{... | collective-permute-start | bytes 1179656 | tf_op jit(solution)/shard_map/conv_reduce/ppermute | solution.py:54
  77.2 12.9 %collective-permute-start.7 = (bf16[128,1536]{1,0:T(8,128)(2,1)S(1)}, bf16[128,1536]{1,0:T(8,128)(2,1)S(1)}, u32[]{:S(2)}, u32[]{:S(2)}) collective-permute-start(bf16[128,1536]{1,0:T(8,128)(2,1)S(1)} %fusion.64), channel_id=1, source_target_pairs={{1,0},{2,1},{3,2},{5,4},{6,5},{7,6},{9,8},{10,9},{11,10},{13,12},{... | collective-permute-start | bytes 1179656 | tf_op jit(solution)/shard_map/conv_reduce/ppermute | solution.py:55
  94.2 11.4 %collective-permute-start.8 = (bf16[128,1536]{1,0:T(8,128)(2,1)}, bf16[128,1536]{1,0:T(8,128)(2,1)S(1)}, u32[]{:S(2)}, u32[]{:S(2)}) collective-permute-start(bf16[128,1536]{1,0:T(8,128)(2,1)} %get-tuple-element.11), channel_id=1, source_target_pairs={{0,1},{1,2},{2,3},{4,5},{5,6},{6,7},{8,9},{9,10},{10,11},{12,13},{... | collective-permute-start | bytes 1179656 | tf_op jit(solution)/shard_map/attn_in_gather/ppermute | solution.py:70
  97.8 12.2 %collective-permute-start.9 = (bf16[128,1536]{1,0:T(8,128)(2,1)}, bf16[128,1536]{1,0:T(8,128)(2,1)S(1)}, u32[]{:S(2)}, u32[]{:S(2)}) collective-permute-start(bf16[128,1536]{1,0:T(8,128)(2,1)} %get-tuple-element.11), channel_id=1, source_target_pairs={{1,0},{2,1},{3,2},{5,4},{6,5},{7,6},{9,8},{10,9},{11,10},{13,12},{... | collective-permute-start | bytes 1179656 | tf_op jit(solution)/shard_map/attn_in_gather/ppermute | solution.py:71
  105.6 10.9 %collective-permute-start.10 = (bf16[128,1536]{1,0:T(8,128)(2,1)S(1)}, bf16[128,1536]{1,0:T(8,128)(2,1)S(1)}, u32[]{:S(2)}, u32[]{:S(2)}) collective-permute-start(bf16[128,1536]{1,0:T(8,128)(2,1)S(1)} %collective-permute-done.8), channel_id=1, source_target_pairs={{0,1},{1,2},{2,3},{4,5},{5,6},{6,7},{8,9},{9,10},{10,11},{12,13},{... | collective-permute-start | bytes 1179656 | tf_op jit(solution)/shard_map/attn_in_gather/ppermute | solution.py:70
  110.0 11.0 %collective-permute-start.11 = (bf16[128,1536]{1,0:T(8,128)(2,1)S(1)}, bf16[128,1536]{1,0:T(8,128)(2,1)S(1)}, u32[]{:S(2)}, u32[]{:S(2)}) collective-permute-start(bf16[128,1536]{1,0:T(8,128)(2,1)S(1)} %collective-permute-done.9), channel_id=1, source_target_pairs={{1,0},{2,1},{3,2},{5,4},{6,5},{7,6},{9,8},{10,9},{11,10},{13,12},{... | collective-permute-start | bytes 1179656 | tf_op jit(solution)/shard_map/attn_in_gather/ppermute | solution.py:71
  116.6 10.1 %collective-permute-start.12 = (bf16[128,1536]{1,0:T(8,128)(2,1)S(1)}, bf16[128,1536]{1,0:T(8,128)(2,1)S(1)}, u32[]{:S(2)}, u32[]{:S(2)}) collective-permute-start(bf16[128,1536]{1,0:T(8,128)(2,1)S(1)} %collective-permute-done.10), channel_id=1, source_target_pairs={{0,1},{1,2},{2,3},{4,5},{5,6},{6,7},{8,9},{9,10},{10,11},{12,13},{... | collective-permute-start | bytes 1179656 | tf_op jit(solution)/shard_map/attn_in_gather/ppermute | solution.py:70
  121.0 9.9 %collective-permute-start.13 = (bf16[128,1536]{1,0:T(8,128)(2,1)S(1)}, bf16[128,1536]{1,0:T(8,128)(2,1)S(1)}, u32[]{:S(2)}, u32[]{:S(2)}) collective-permute-start(bf16[128,1536]{1,0:T(8,128)(2,1)S(1)} %collective-permute-done.11), channel_id=1, source_target_pairs={{1,0},{2,1},{3,2},{5,4},{6,5},{7,6},{9,8},{10,9},{11,10},{13,12},{... | collective-permute-start | bytes 1179656 | tf_op jit(solution)/shard_map/attn_in_gather/ppermute | solution.py:71
  134.7 8.7 %collective-permute-start.14 = (bf16[2,512,256]{2,1,0:T(8,128)(2,1)S(1)}, bf16[2,512,256]{2,1,0:T(8,128)(2,1)S(1)}, u32[]{:S(2)}, u32[]{:S(2)}) collective-permute-start(bf16[2,512,256]{2,1,0:T(8,128)(2,1)S(1)} %slice.92), channel_id=1, source_target_pairs={{0,4},{4,8},{8,12},{12,0},{1,5},{5,9},{9,13},{13,1},{2,6},{6,10},{... | collective-permute-start | bytes 1572872 | tf_op jit(solution)/shard_map/kv_ring/ppermute | solution.py:154
  143.3 8.6 %collective-permute-start.15 = (bf16[2,512,256]{2,1,0:T(8,128)(2,1)S(1)}, bf16[2,512,256]{2,1,0:T(8,128)(2,1)S(1)}, u32[]{:S(2)}, u32[]{:S(2)}) collective-permute-start(bf16[2,512,256]{2,1,0:T(8,128)(2,1)S(1)} %collective-permute-done.14), channel_id=1, source_target_pairs={{0,4},{4,8},{8,12},{12,0},{1,5},{5,9},{9,13},{13,1},{2,6},{6,10},{... | collective-permute-start | bytes 1572872 | tf_op jit(solution)/shard_map/kv_ring/ppermute | solution.py:154
  151.9 8.6 %collective-permute-start.16 = (bf16[2,512,256]{2,1,0:T(8,128)(2,1)S(1)}, bf16[2,512,256]{2,1,0:T(8,128)(2,1)S(1)}, u32[]{:S(2)}, u32[]{:S(2)}) collective-permute-start(bf16[2,512,256]{2,1,0:T(8,128)(2,1)S(1)} %collective-permute-done.15), channel_id=1, source_target_pairs={{0,4},{4,8},{8,12},{12,0},{1,5},{5,9},{9,13},{13,1},{2,6},{6,10},{... | collective-permute-start | bytes 1572872 | tf_op jit(solution)/shard_map/kv_ring/ppermute | solution.py:154
  167.6 10.6 %collective-permute-start.17 = (bf16[128,1536]{1,0:T(8,128)(2,1)S(1)}, bf16[128,1536]{1,0:T(8,128)(2,1)S(1)}, u32[]{:S(2)}, u32[]{:S(2)}) collective-permute-start(bf16[128,1536]{1,0:T(8,128)(2,1)S(1)} %get-tuple-element.16), channel_id=1, source_target_pairs={{0,1},{1,2},{2,3},{4,5},{5,6},{6,7},{8,9},{9,10},{10,11},{12,13},{... | collective-permute-start | bytes 1179656 | tf_op jit(solution)/shard_map/out_reduce/ppermute | solution.py:54
  169.9 12.9 %collective-permute-start.20 = (bf16[128,1536]{1,0:T(8,128)(2,1)S(1)}, bf16[128,1536]{1,0:T(8,128)(2,1)S(1)}, u32[]{:S(2)}, u32[]{:S(2)}) collective-permute-start(bf16[128,1536]{1,0:T(8,128)(2,1)S(1)} %get-tuple-element.17), channel_id=1, source_target_pairs={{1,0},{2,1},{3,2},{5,4},{6,5},{7,6},{9,8},{10,9},{11,10},{13,12},{... | collective-permute-start | bytes 1179656 | tf_op jit(solution)/shard_map/out_reduce/ppermute | solution.py:55
  178.4 11.7 %collective-permute-start.18 = (bf16[128,1536]{1,0:T(8,128)(2,1)S(1)}, bf16[128,1536]{1,0:T(8,128)(2,1)S(1)}, u32[]{:S(2)}, u32[]{:S(2)}) collective-permute-start(bf16[128,1536]{1,0:T(8,128)(2,1)S(1)} %fusion.58), channel_id=1, source_target_pairs={{0,1},{1,2},{2,3},{4,5},{5,6},{6,7},{8,9},{9,10},{10,11},{12,13},{... | collective-permute-start | bytes 1179656 | tf_op jit(solution)/shard_map/out_reduce/ppermute | solution.py:54
  190.3 12.0 %collective-permute-start.21 = (bf16[128,1536]{1,0:T(8,128)(2,1)S(1)}, bf16[128,1536]{1,0:T(8,128)(2,1)S(1)}, u32[]{:S(2)}, u32[]{:S(2)}) collective-permute-start(bf16[128,1536]{1,0:T(8,128)(2,1)S(1)} %get-tuple-element.15), channel_id=1, source_target_pairs={{1,0},{2,1},{3,2},{5,4},{6,5},{7,6},{9,8},{10,9},{11,10},{13,12},{... | collective-permute-start | bytes 1179656 | tf_op jit(solution)/shard_map/out_reduce/ppermute | solution.py:55
  191.7 12.1 %collective-permute-start.19 = (bf16[128,1536]{1,0:T(8,128)(2,1)S(1)}, bf16[128,1536]{1,0:T(8,128)(2,1)S(1)}, u32[]{:S(2)}, u32[]{:S(2)}) collective-permute-start(bf16[128,1536]{1,0:T(8,128)(2,1)S(1)} %get-tuple-element.14), channel_id=1, source_target_pairs={{0,1},{1,2},{2,3},{4,5},{5,6},{6,7},{8,9},{9,10},{10,11},{12,13},{... | collective-permute-start | bytes 1179656 | tf_op jit(solution)/shard_map/out_reduce/ppermute | solution.py:54
  202.4 9.8 %collective-permute-start.22 = (bf16[128,1536]{1,0:T(8,128)(2,1)S(1)}, bf16[128,1536]{1,0:T(8,128)(2,1)S(1)}, u32[]{:S(2)}, u32[]{:S(2)}) collective-permute-start(bf16[128,1536]{1,0:T(8,128)(2,1)S(1)} %fusion.57), channel_id=1, source_target_pairs={{1,0},{2,1},{3,2},{5,4},{6,5},{7,6},{9,8},{10,9},{11,10},{13,12},{... | collective-permute-start | bytes 1179656 | tf_op jit(solution)/shard_map/out_reduce/ppermute | solution.py:55
  (13 other events, 301.7 us)
